TPU v7x, 256 devices: a whole 4x4x8 slice. The times are simulated.
256 devices in a mesh: cfg: 2 (over z_lo), seq: 16 (over z_hi, x), wblk: 8 (over y, core).
Axes of the slice: x: 4, y: 4, z: 8 (z_hi: 4, z_lo: 2; z = z_hi * 2 + z_lo), core: 2. Of those that a mesh axis runs over, the one named last changes fastest.
Arguments:
- text_tokens: bfloat16 [2, 2, 512, 3072], P('cfg', None, 'seq', 'wblk'), may hold values from -16 to 16
- image_tokens: bfloat16 [2, 4096, 3072], P(None, 'seq', 'wblk'), may hold values from -16 to 16
- pooled_vector: float32 [2, 3072], P('cfg', 'seq'), may hold values from -6 to 6
- mod_weight: bfloat16 [3072, 3, 3072], P('seq', None, 'wblk'), may hold values from -0.109375 to 0.109375
- qkv_weight: bfloat16 [3072, 3, 16, 128], P('seq', None, 'wblk'), may hold values from -0.109375 to 0.109375
- up_weight: bfloat16 [3072, 6144], P('seq', 'wblk'), may hold values from -0.109375 to 0.109375
- query_gain: float32 [128], replicated, may hold values from 0.6 to 10
- key_gain: float32 [128], replicated, may hold values from 0.6 to 10
- attn_weight: bfloat16 [2048, 3072], P('wblk', 'seq'), may hold values from -0.125 to 0.125
- down_weight: bfloat16 [6144, 3072], P('wblk', 'seq'), may hold values from -0.078125 to 0.078125
- lengths: int32 [2], replicated, may hold values from 1 to 512, as said below
- timestep: int32 [1], replicated, may hold values from 0 to 27
Outputs:
- text_out: bfloat16 [2, 2, 512, 3072], P('cfg', None, 'seq', 'wblk')
- velocity: float32 [2, 4096, 3072], P('cfg', 'seq', 'wblk')
- new_image: float32 [2, 4096, 3072], P('cfg', 'seq', 'wblk')
Inputs may be any that keep to these rules, and one draw needn't show every extreme that they name: `lengths`: some prompt has all 512 text tokens live in every draw.
All inputs are finite; a program needn't handle non-finite values.
Results may differ from a plain program's by a relative error of at most 0.025.
Values may be sent and summed in bfloat16 or wider, within the bound.
No kernel may reach another device: no remote copies, remote signals or barrier semaphores. Data moves between devices by JAX's collectives and lax.ppermute only.
A program may use at most 128 MiB of HBM per device.

v0:
```python
import math
import jax
import jax.numpy as jnp
from jax import lax
from jax.sharding import PartitionSpec as P

D = 3072
HD = 128
GRID = 64
STEPS = 28
epsilon = 1e-06
guidance = 3.5
time_shift = 3.0
rope_theta = 10000.0


def plan(timestep):
    step_index = timestep[0].astype(jnp.float32)
    time_now = 1.0 - step_index / STEPS
    time_next = 1.0 - (step_index + 1.0) / STEPS
    sigma_now = time_shift * time_now / (1.0 + (time_shift - 1.0) * time_now)
    sigma_next = time_shift * time_next / (1.0 + (time_shift - 1.0) * time_next)
    return (sigma_now, sigma_next - sigma_now)


def time_embedding(sigma_now, dim_count):
    halfwidth = dim_count // 2
    frequency = jnp.exp(-math.log(10000.0) * jnp.arange(halfwidth, dtype=jnp.float32) / halfwidth)
    angles = 1000.0 * sigma_now * frequency
    return jnp.concatenate([jnp.cos(angles), jnp.sin(angles)])


def inverse_freq(dim_count):
    return rope_theta ** (-jnp.arange(0, dim_count, 2, dtype=jnp.float32) / dim_count)


def rotary_angles(height_pos, width_pos):
    still_dims = HD // 8
    axis_dims = (HD - still_dims) // 2
    return jnp.concatenate(
        [
            jnp.zeros((height_pos.shape[0], still_dims // 2), jnp.float32),
            height_pos[:, None] * inverse_freq(axis_dims)[None],
            width_pos[:, None] * inverse_freq(axis_dims)[None],
        ],
        axis=1,
    )


def rotate(vectors, angles):
    paired_dims = vectors.reshape(vectors.shape[:-1] + (HD // 2, 2))
    cosine_table = jnp.cos(angles)[:, None, :]
    sine_table = jnp.sin(angles)[:, None, :]
    first_part = paired_dims[..., 0]
    second_part = paired_dims[..., 1]
    turned = jnp.stack(
        [
            first_part * cosine_table - second_part * sine_table,
            first_part * sine_table + second_part * cosine_table,
        ],
        axis=-1,
    )
    return turned.reshape(vectors.shape)


def head_norm(vectors, gain_vector):
    return (
        vectors
        * lax.rsqrt(jnp.mean(vectors * vectors, axis=-1, keepdims=True) + epsilon)
        * gain_vector
    )


def input_folder(source, pieces):
    width_rows = pieces[0].shape[0]
    first_total = jnp.dot(
        source, pieces[0].reshape(width_rows, -1), preferred_element_type=jnp.float32
    )
    second_total = jnp.dot(source, pieces[1], preferred_element_type=jnp.float32)
    return (first_total, second_total)


def output_folder(attended, activated, pieces):
    block_cols = jnp.dot(attended, pieces[0], preferred_element_type=jnp.float32)
    block_cols = block_cols + jnp.dot(activated, pieces[1], preferred_element_type=jnp.float32)
    return block_cols


def shards(
    text_tokens,
    image_tokens,
    pooled_vector,
    mod_weight,
    qkv_weight,
    up_weight,
    query_gain,
    key_gain,
    attn_weight,
    down_weight,
    lengths,
    timestep,
):
    seq_pos = lax.axis_index("seq")
    cfg_pos = lax.axis_index("cfg")
    prompts = image_tokens.shape[0]
    image_rows = image_tokens.shape[1]
    text_rows = text_tokens.shape[2]
    local_len = text_rows + image_rows
    dim_local = image_tokens.shape[2]
    dim_seq = pooled_vector.shape[1]
    heads_local = qkv_weight.shape[2]
    row_count = prompts * local_len
    sigma_now, step_size = plan(timestep)
    embedded = lax.dynamic_slice_in_dim(time_embedding(sigma_now, D), seq_pos * dim_seq, dim_seq)
    cond_vec = jax.nn.silu(pooled_vector[0] + embedded).astype(jnp.bfloat16)[None]
    mod_terms = jnp.dot(
        cond_vec, mod_weight.reshape(dim_seq, 3 * dim_local), preferred_element_type=jnp.float32
    )
    modulation = lax.psum(mod_terms.reshape(3, dim_local), "seq")
    local_rows = jnp.concatenate([text_tokens[0], image_tokens], axis=1)
    hidden = local_rows.astype(jnp.float32)
    totals, squares = lax.psum(
        (jnp.sum(hidden, axis=-1), jnp.sum(hidden * hidden, axis=-1)), "wblk"
    )
    average = (totals / D)[..., None]
    variance = (squares / D)[..., None] - average * average
    normed = (
        (hidden - average) * lax.rsqrt(variance + epsilon) * (1.0 + modulation[1]) + modulation[0]
    ).astype(jnp.bfloat16)
    gathered = lax.all_gather(normed, "wblk", axis=2, tiled=True)
    token_rows = gathered.reshape(row_count, D)
    projected, mlp_units = input_folder(
        token_rows,
        (
            lax.all_gather(qkv_weight, "seq", axis=0, tiled=True),
            lax.all_gather(up_weight, "seq", axis=0, tiled=True),
        ),
    )
    projected = projected.reshape(prompts, local_len, 3, heads_local, HD)
    image_index = seq_pos * image_rows + jnp.arange(image_rows, dtype=jnp.int32)
    height_pos = jnp.concatenate(
        [jnp.zeros((text_rows,), jnp.float32), (image_index // GRID).astype(jnp.float32)]
    )
    width_pos = jnp.concatenate(
        [jnp.zeros((text_rows,), jnp.float32), (image_index % GRID).astype(jnp.float32)]
    )
    angles = rotary_angles(height_pos, width_pos)
    queries = rotate(head_norm(projected[:, :, 0], query_gain), angles).astype(jnp.bfloat16)
    key_rows = rotate(head_norm(projected[:, :, 1], key_gain), angles).astype(jnp.bfloat16)
    values = projected[:, :, 2].astype(jnp.bfloat16)
    scale_factor = HD ** (-0.5)
    running_max = jnp.full((prompts, heads_local, local_len), -1e30, jnp.float32)
    key_piece = lax.all_gather(key_rows, "seq", axis=1, tiled=True)
    value_piece = lax.all_gather(values, "seq", axis=1, tiled=True)
    width_keys = key_piece.shape[1]
    where_global = jnp.arange(width_keys, dtype=jnp.int32)
    shard_index = where_global // local_len
    within = where_global % local_len
    text_index = shard_index * text_rows + within
    key_live = (within >= text_rows)[None, :] | (text_index[None, :] < lengths[:, None])
    scores = (
        jnp.einsum("pqhd,pkhd->phqk", queries, key_piece, preferred_element_type=jnp.float32)
        * scale_factor
    )
    scores = jnp.where(key_live[:, None, None, :], scores, -1e30)
    new_max = jnp.maximum(running_max, jnp.max(scores, axis=-1))
    weights = jnp.exp(scores - new_max[..., None])
    denominator = jnp.sum(weights, axis=-1)
    numerator = jnp.einsum(
        "phqk,pkhd->phqd",
        weights.astype(jnp.bfloat16),
        value_piece,
        preferred_element_type=jnp.float32,
    )
    running_max, denominator, numerator = (new_max, denominator, numerator)
    attended = (numerator / denominator[..., None]).astype(jnp.bfloat16)
    attended = attended.transpose(0, 2, 1, 3).reshape(row_count, heads_local * HD)
    activated = jax.nn.gelu(mlp_units, approximate=True).astype(jnp.bfloat16)
    branch_terms = output_folder(
        attended,
        activated,
        (
            lax.all_gather(attn_weight, "seq", axis=1, tiled=True),
            lax.all_gather(down_weight, "seq", axis=1, tiled=True),
        ),
    )
    branch = lax.psum_scatter(
        branch_terms.reshape(prompts, local_len, D).astype(jnp.bfloat16),
        "wblk",
        scatter_dimension=2,
        tiled=True,
    ).astype(jnp.float32)
    layer_out = hidden + modulation[2] * branch
    text_out = layer_out[:, :text_rows].astype(jnp.bfloat16)[None]
    image_out = layer_out[:, text_rows:]
    paired = lax.all_to_all(
        image_out[:, None].astype(jnp.bfloat16), "cfg", split_axis=0, concat_axis=1, tiled=True
    ).astype(jnp.float32)
    velocity = paired[:, 1] + guidance * (paired[:, 0] - paired[:, 1])
    own_prompts = prompts // 2
    latent = lax.dynamic_slice_in_dim(image_tokens, cfg_pos * own_prompts, own_prompts, 0).astype(
        jnp.float32
    )
    new_image = latent + step_size * velocity
    return (text_out, velocity, new_image)


def solution(mesh):
    in_specs = (
        P("cfg", None, "seq", "wblk"),
        P(None, "seq", "wblk"),
        P("cfg", "seq"),
        P("seq", None, "wblk"),
        P("seq", None, "wblk", None),
        P("seq", "wblk"),
        P(),
        P(),
        P("wblk", "seq"),
        P("wblk", "seq"),
        P(),
        P(),
    )
    out_specs = (P("cfg", None, "seq", "wblk"), P("cfg", "seq", "wblk"), P("cfg", "seq", "wblk"))
    return jax.shard_map(shards, mesh=mesh, in_specs=in_specs, out_specs=out_specs, check_vma=False)
```

profile of v0, /device:TPU:2, one launch (start us, length us, event | category | flops | bytes accessed | tf_op | source)
XLA Modules:
  0.0 606.9 jit_solution(16747836014548433341)
XLA Ops:
  8.7 0.8 fusion.73
  9.7 1.3 convert_reduce_fusion
  11.0 15.1 %all-reduce.2 = (f32[2,288]{1,0:T(2,128)S(1)}, f32[2,288]{1,0:T(2,128)S(1)}) all-reduce(f32[2,288]{1,0:T(2,128)S(1)} %get-tuple-element.6, f32[2,288]{1,0:T(2,128)S(1)} %get-tuple-element.5), channel_id=1, replica_groups=mesh['cfg'=2,'seq'=16,'wblk'=8] {'wblk'}, use_global_device_ids=true, to_apply=%region_4.5 | all-reduce | flops 1152 | bytes 9216 | tf_op jit(solution)/shard_map/psum | solution.py:122
  26.1 46.2 %psum.21 = f32[3,384]{1,0:T(4,128)S(1)} all-reduce(f32[3,384]{1,0:T(4,128)S(1)} %bitcast.105), channel_id=1, replica_groups=mesh['cfg'=2,'seq'=16,'wblk'=8] {'seq'}, use_global_device_ids=true, to_apply=%region_0.1 | all-reduce | flops 1152 | bytes 9216 | tf_op jit(solution)/shard_map/psum | solution.py:119
  72.4 2.0 fusion.36
  75.8 0.8 mul.324
  76.6 0.8 mul.305
  78.1 13.8 %all-gather.11.cloned.1.call-done = bf16[3072,3,2,128]{3,2,1,0:T(2,128)(2,1)} async-done(((bf16[192,3,2,128]{3,2,1,0:T(2,128)(2,1)}), bf16[3072,3,2,128]{3,2,1,0:T(2,128)(2,1)}) %all-gather.11.cloned.1.call-update) | async-done | bytes 4718608 | tf_op jit(solution)/shard_map/all_gather | solution.py:135
  91.9 12.5 %copy.34 = bf16[3072,3,2,128]{0,3,2,1:T(8,128)(2,1)} copy(bf16[3072,3,2,128]{3,2,1,0:T(2,128)(2,1)} %all-gather.11.cloned.1.call-done) | data formatting | bytes 9437184 | tf_op jit(solution)/shard_map/reshape | solution.py:77
  104.4 23.5 %all-gather.9.cloned.1.call-done = bf16[2,288,3072]{2,1,0:T(8,128)(2,1)} async-done(((bf16[2,288,384]{2,1,0:T(8,128)(2,1)}), bf16[2,288,3072]{2,1,0:T(8,128)(2,1)}) %all-gather.9.cloned.1.call-update) | async-done | bytes 3538960 | tf_op jit(solution)/shard_map/all_gather | solution.py:130
  127.9 6.8 %fusion.6 = f32[2,288,3,2,128]{4,1,3,2,0:T(8,128)S(1)} fusion(bf16[3072,3,2,128]{0,3,2,1:T(8,128)(2,1)} %copy.34, bf16[2,288,3072]{2,1,0:T(8,128)(2,1)} %all-gather.9.cloned.1.call-done), kind=kOutput, calls=%fused_computation.8 | convolution fusion | flops 2717908992 | bytes 10027008 | tf_op jit(solution)/shard_map/dot_general | solution.py:76
  137.7 0.8 subtract_convert_fusion.1
  139.1 1.1 copy.27
  140.2 1.8 slice.102
  143.8 64.8 %all-gather.17.cloned.1.call-done = bf16[3072,768]{1,0:T(8,128)(2,1)} async-done(((bf16[192,768]{1,0:T(8,128)(2,1)}), bf16[3072,768]{1,0:T(8,128)(2,1)}) %all-gather.17.cloned.1.call-update) | async-done | bytes 4718608 | tf_op jit(solution)/shard_map/all_gather | solution.py:136
  208.6 82.8 %all-gather.19.cloned.1.call-done = bf16[768,3072]{0,1:T(8,128)(2,1)} async-done(((bf16[768,192]{0,1:T(8,128)(2,1)}), bf16[768,3072]{0,1:T(8,128)(2,1)}) %all-gather.19.cloned.1.call-update) | async-done | bytes 4718608 | tf_op jit(solution)/shard_map/all_gather | solution.py:184
  291.5 15.0 %fusion.39 = f32[576,3072]{1,0:T(8,128)} fusion(bf16[768,3072]{0,1:T(8,128)(2,1)} %all-gather.19.cloned.1.call-done, bf16[576,3072]{1,0:T(8,128)(2,1)} %bitcast.108, bf16[3072,768]{1,0:T(8,128)(2,1)} %all-gather.17.cloned.1.call-done), kind=kOutput, calls=%fused_computation.34 | convolution fusion | flops 5439799296 | bytes 20054016 | tf_op jit(solution)/shard_map/dot_general | solution.py:85
  306.5 68.4 %all-gather.13.cloned.1.call-done = bf16[2,4608,2,128]{3,1,2,0:T(8,128)(2,1)} async-done(((bf16[2,288,2,128]{3,1,2,0:T(8,128)(2,1)}), bf16[2,4608,2,128]{3,1,2,0:T(8,128)(2,1)}) %all-gather.13.cloned.1.call-update) | async-done | bytes 4718608 | tf_op jit(solution)/shard_map/all_gather | solution.py:153
  374.9 13.5 %fusion = (f32[2,2,288]{2,1,0:T(2,128)S(1)}, f32[2,2,288,4608]{3,2,1,0:T(8,128)}) fusion(pred[2,4608]{1,0:T(4,128)(4,1)S(1)} %compare_or_fusion, bf16[2,4608,2,128]{3,1,2,0:T(8,128)(2,1)} %all-gather.13.cloned.1.call-done, bf16[2,288,2,128]{1,2,3,0:T(2,128)(2,1)S(1)} %bitcast.100), kind=kOutput, calls=%fused_computation.2 | convolution fusion | flops 1374878592 | bytes 26260992 | tf_op jit(solution)/shard_map/pqhd,pkhd->phqk/dot_general | solution.py:162
  388.4 10.3 %fusion.1 = f32[2,2,288]{2,1,0:T(2,128)S(1)} fusion(f32[2,2,288,4608]{3,2,1,0:T(8,128)} %get-tuple-element.29, f32[2,2,288]{2,1,0:T(2,128)S(1)} %broadcast_maximum_fusion, pred[2,4608]{1,0:T(4,128)(4,1)S(1)} %compare_or_fusion), kind=kLoop, calls=%fused_computation.3 | loop fusion | flops 21232512 | bytes 21252096 | tf_op jit(solution)/shard_map/reduce_sum | solution.py:168
  398.7 59.5 %all-gather.21.cloned.1.call-done = bf16[2,4608,1,2,128]{4,1,3,2,0:T(8,128)(2,1)} async-done(((bf16[2,288,1,2,128]{4,1,3,2,0:T(8,128)(2,1)}), bf16[2,4608,1,2,128]{4,1,3,2,0:T(8,128)(2,1)}) %all-gather.21.cloned.1.call-update) | async-done | bytes 4718608 | tf_op jit(solution)/shard_map/all_gather | solution.py:154
  458.3 10.9 %fusion.28 = bf16[2,288,2,128]{3,1,2,0:T(8,128)(2,1)S(1)} fusion(bf16[2,4608,1,2,128]{4,1,3,2,0:T(8,128)(2,1)} %all-gather.21.cloned.1.call-done, f32[2,2,288,4608]{3,2,1,0:T(8,128)} %get-tuple-element.29, f32[2,2,288]{2,1,0:T(2,128)S(1)} %broadcast_maximum_fusion, pred[2,4608]{1,0:T(4,128)(4,1)S(1)} %compare_or_fusion, f32[2,288,2]{1,2,0:T(2,128)S(1)} %bitcast.106), kind=kOutput, calls=%fused_computation.27 | convolution fusion | flops 1380483072 | bytes 26265600 | tf_op jit(solution)/shard_map/phqk,pkhd->phqd/dot_general | solution.py:169
  469.5 50.2 %all-gather.15.cloned.1.call-done = bf16[256,3072]{0,1:T(8,128)(2,1)} async-done(((bf16[256,192]{0,1:T(8,128)(2,1)}), bf16[256,3072]{0,1:T(8,128)(2,1)}) %all-gather.15.cloned.1.call-update) | async-done | bytes 1572880 | tf_op jit(solution)/shard_map/all_gather | solution.py:183
  519.6 6.4 %add_convert_fusion = bf16[576,3072]{1,0:T(8,128)(2,1)} fusion(f32[576,3072]{1,0:T(8,128)} %fusion.39, bf16[256,3072]{0,1:T(8,128)(2,1)} %all-gather.15.cloned.1.call-done, bf16[72,8,2,128]{3,2,1,0:T(2,128)(2,1)S(1)} %bitcast.101), kind=kOutput, calls=%fused_computation.7 | convolution fusion | flops 909508608 | bytes 12484608 | tf_op jit(solution)/shard_map/dot_general | solution.py:84
  526.0 12.3 %copy.35 = bf16[2,288,3072]{1,0,2:T(2,128)(2,1)} copy(bf16[2,288,3072]{2,1,0:T(8,128)(2,1)} %bitcast.95) | data formatting | bytes 7077888
  538.3 10.2 %reshape.323 = bf16[3072,576]{1,0:T(8,128)(2,1)} reshape(bf16[3072,2,288]{2,1,0:T(2,128)(2,1)} %bitcast.94) | data formatting | bytes 7077888
  548.5 37.4 %reduce-scatter.4.cloned.1.call-done = bf16[384,576]{1,0:T(8,128)(2,1)} async-done(((bf16[3072,576]{1,0:T(8,128)(2,1)}), bf16[384,576]{1,0:T(8,128)(2,1)}) %reduce-scatter.4.cloned.1.call-update) | async-done | bytes 442384
  585.9 2.1 reshape.324
  588.9 0.8 slice_bitcast_fusion.2
  589.7 3.5 all-to-all-start
  593.8 5.2 all-to-all-done
  599.1 1.0 multiply_add_fusion
  (60 shorter events, 10.1 us)
Async XLA Ops:
  7.2 2.3 copy-start
  7.2 84.7 %all-gather.11.cloned.1.call-start = ((), (), s32[]{:S(2)}) async-start(), calls=%async_computation.3 | async-start | bytes 5013504 | tf_op jit(solution)/shard_map/all_gather | solution.py:135
  7.9 120.0 %all-gather.9.cloned.1.call-start = ((), (), s32[]{:S(2)}) async-start(), calls=%async_computation.2 | async-start | bytes 3981312 | tf_op jit(solution)/shard_map/all_gather | solution.py:130
  74.4 134.2 %all-gather.17.cloned.1.call-start = ((), (), s32[]{:S(2)}) async-start(), calls=%async_computation.6 | async-start | bytes 5013504 | tf_op jit(solution)/shard_map/all_gather | solution.py:136
  75.2 216.3 %all-gather.19.cloned.1.call-start = ((), (), s32[]{:S(2)}) async-start(), calls=%async_computation.7 | async-start | bytes 5013504 | tf_op jit(solution)/shard_map/all_gather | solution.py:184
  75.7 299.1 %all-gather.13.cloned.1.call-start = ((), (), s32[]{:S(2)}) async-start(), calls=%async_computation.4 | async-start | bytes 5013504 | tf_op jit(solution)/shard_map/all_gather | solution.py:153
  134.6 1.2 copy-start.3
  136.4 6.7 %copy-start.5 = (s32[2]{0:T(128)S(1)}, s32[2]{0:T(128)}, u32[]{:S(2)}) copy-start(s32[2]{0:T(128)} %param.22) | copy-start | bytes 28
  140.2 318.1 %all-gather.21.cloned.1.call-start = ((), (), s32[]{:S(2)}) async-start(), calls=%async_computation.8 | async-start | bytes 5013504 | tf_op jit(solution)/shard_map/all_gather | solution.py:154
  142.1 377.6 %all-gather.15.cloned.1.call-start = ((), (), s32[]{:S(2)}) async-start(), calls=%async_computation.5 | async-start | bytes 1671168 | tf_op jit(solution)/shard_map/all_gather | solution.py:183
  142.8 443.1 %reduce-scatter.4.cloned.1.call-start = ((), (), s32[]{:S(2)}) async-start(), calls=%async_computation.9 | async-start | bytes 4423680
  548.5 40.2 %copy-start.2 = (bf16[2,256,384]{2,1,0:T(8,128)(2,1)S(1)}, bf16[2,256,384]{2,1,0:T(8,128)(2,1)}, u32[]{:S(2)}) copy-start(bf16[2,256,384]{2,1,0:T(8,128)(2,1)} %param.13) | copy-start | bytes 1179652
  548.5 40.3 %copy-start.4 = (bf16[1,2,32,384]{3,2,1,0:T(8,128)(2,1)S(1)}, bf16[1,2,32,384]{3,2,1,0:T(8,128)(2,1)}, u32[]{:S(2)}) copy-start(bf16[1,2,32,384]{3,2,1,0:T(8,128)(2,1)} %param.12) | copy-start | bytes 147460
  548.5 51.5 %copy-start.1 = (bf16[192,3,384]{2,0,1:T(8,128)(2,1)S(1)}, bf16[192,3,384]{2,0,1:T(8,128)(2,1)}, u32[]{:S(2)}) copy-start(bf16[192,3,384]{2,0,1:T(8,128)(2,1)} %param.15) | copy-start | bytes 1327108
  589.7 9.3 %all-to-all-start = ((bf16[2,1,256,384]{3,2,1,0:T(8,128)(2,1)}), bf16[2,1,256,384]{3,2,1,0:T(8,128)(2,1)S(1)}, u32[]{:S(2)}, u32[]{:S(2)}) async-start(bf16[2,1,256,384]{3,2,1,0:T(8,128)(2,1)} %slice_bitcast_fusion.2), calls=%async_computation | async-start | bytes 786432 | tf_op jit(solution)/shard_map/all_to_all | solution.py:196
Sparse Core Ops, SparseCore 0:
  10.4 81.3 all-gather.10
  93.7 34.1 all-gather.8
  130.3 78.2 all-gather.16
  210.9 80.5 all-gather.18
  294.3 80.5 all-gather.12
  377.7 80.5 all-gather.20
  460.7 58.8 all-gather.14
  548.6 37.2 reduce-scatter.3
where the time goes:
time: 608 us; the launch traced here: 607 us
  waiting for transfers between devices  408 us (67%)
  blocking collectives  61.3 us (10%)
  matrix products  52.8 us (9%)
  local copies, waits for them, and re-layouts  45.8 us (8%)
  other arithmetic  19.5 us (3%)
  between operations  15.2 us (2%)
    all_gather x1, waiting for transfers between devices, shards(): lax.all_gather(down_weight, 'seq', axis=1, tiled=True)  82.8 us
    all_gather x1, waiting for transfers between devices, shards(): key_piece = lax.all_gather(key_rows, 'seq', axis=1, tiled=True)  68.4 us
    all_gather x1, waiting for transfers between devices, shards(): lax.all_gather(up_weight, 'seq', axis=0, tiled=True)  64.8 us
    all_gather x1, waiting for transfers between devices, shards(): value_piece = lax.all_gather(values, 'seq', axis=1, tiled=True)  59.5 us
    all_gather x1, waiting for transfers between devices, shards(): lax.all_gather(attn_weight, 'seq', axis=1, tiled=True)  50.2 us
    psum x1, blocking collectives, shards(): modulation = lax.psum(mod_terms.reshape(3, dim_local), 'seq')  46.2 us
    unnamed x9, waiting for transfers between devices  40 us
    unnamed x16, local copies, waits for them, and re-layouts  26 us
  transfers between devices with their start and end apart: 9, of which 9 were waited for; matrix products, arithmetic and copies ran while one was open for 14% of the time, Pallas kernels for 0%

commit v1 on v0

--- a/solution.py
+++ b/solution.py
@@ -12,6 +12,25 @@
 guidance = 3.5
 time_shift = 3.0
 rope_theta = 10000.0
+
+
+def collect(array, axis, dim):
+    size, mine, rows = (lax.axis_size(axis), lax.axis_index(axis), array.shape[dim])
+    forward = [(i, (i + 1) % size) for i in range(size)]
+    behind = [(i, (i - 1) % size) for i in range(size)]
+    out = jnp.zeros((*array.shape[:dim], size * rows, *array.shape[dim + 1 :]), array.dtype)
+    out = lax.dynamic_update_slice_in_dim(out, array, mine * rows, axis=dim)
+    from_left = from_right = array
+    half = size // 2
+    for hop in range(1, half + 1):
+        from_left = lax.ppermute(from_left, axis, forward)
+        out = lax.dynamic_update_slice_in_dim(out, from_left, (mine - hop) % size * rows, axis=dim)
+        if hop < size - half:
+            from_right = lax.ppermute(from_right, axis, behind)
+            out = lax.dynamic_update_slice_in_dim(
+                out, from_right, (mine + hop) % size * rows, axis=dim
+            )
+    return out
 
 
 def plan(timestep):
@@ -127,7 +146,7 @@
     normed = (
         (hidden - average) * lax.rsqrt(variance + epsilon) * (1.0 + modulation[1]) + modulation[0]
     ).astype(jnp.bfloat16)
-    gathered = lax.all_gather(normed, "wblk", axis=2, tiled=True)
+    gathered = collect(normed, "wblk", 2)
     token_rows = gathered.reshape(row_count, D)
     projected, mlp_units = input_folder(
         token_rows,

time: 608 us -> 575 us (0.946)
  waiting for transfers between devices: 408 us -> 361 us
  starting transfers between devices: 3.96 us -> 13.1 us
  local copies, waits for them, and re-layouts: 45.8 us -> 52.7 us
    all_gather x1, waiting for transfers between devices: 64.8 us -> 34.5 us  [shards(): lax.all_gather(up_weight, 'seq', axis=0, tiled=True)]
    all_gather x1 -> x0, waiting for transfers between devices: 23.5 us -> none  [shards(): gathered = lax.all_gather(normed, 'wblk', axis=2, tiled=True)]
    ppermute x0 -> x7, waiting for transfers between devices: none -> 20.3 us  [the longest x4 20.3 us: collect(): from_left = lax.ppermute(from_left, axis, forward)]
    all_gather x1, waiting for transfers between devices: 13.8 us -> 0.01 us  [shards(): lax.all_gather(qkv_weight, 'seq', axis=0, tiled=True)]
    ppermute x0 -> x7, starting transfers between devices: none -> 9.17 us  [the longest x3 9.16 us: collect(): from_right = lax.ppermute(from_right, axis, behind)]
    unnamed x16 -> x20, local copies, waits for them, and re-layouts: 26 us -> 26 us
    unnamed x9 -> x8, waiting for transfers between devices: 40 us -> 40 us
  transfers between devices with their start and end apart: 9 -> 15, of which waited for: 9 -> 11; matrix products, arithmetic and copies ran while one was open for 14% -> 16% of each run, Pallas kernels for 0% -> 0%
where the time goes in v1:
time: 575 us; the launch traced here: 573 us
  waiting for transfers between devices  361 us (63%)
  blocking collectives  59.7 us (10%)
  matrix products  52.8 us (9%)
  local copies, waits for them, and re-layouts  52.7 us (9%)
  other arithmetic  18.6 us (3%)
  between operations  15.3 us (3%)
  starting transfers between devices  13.1 us (2%)
    all_gather x1, waiting for transfers between devices, shards(): lax.all_gather(down_weight, 'seq', axis=1, tiled=True)  83 us
    all_gather x1, waiting for transfers between devices, shards(): key_piece = lax.all_gather(key_rows, 'seq', axis=1, tiled=True)  68.4 us
    all_gather x1, waiting for transfers between devices, shards(): value_piece = lax.all_gather(values, 'seq', axis=1, tiled=True)  59.5 us
    all_gather x1, waiting for transfers between devices, shards(): lax.all_gather(attn_weight, 'seq', axis=1, tiled=True)  50 us
    psum x1, blocking collectives, shards(): modulation = lax.psum(mod_terms.reshape(3, dim_local), 'seq')  44.7 us
    unnamed x8, waiting for transfers between devices  40 us
    all_gather x1, waiting for transfers between devices, shards(): lax.all_gather(up_weight, 'seq', axis=0, tiled=True)  34.5 us
    unnamed x20, local copies, waits for them, and re-layouts  26 us
  transfers between devices with their start and end apart: 15, of which 11 were waited for; matrix products, arithmetic and copies ran while one was open for 16% of the time, Pallas kernels for 0%

profile of v1, /device:TPU:2, one launch (start us, length us, event | category | flops | bytes accessed | tf_op | source)
XLA Modules:
  0.0 573.3 jit_solution(8886834452780840313)
XLA Ops:
  11.2 1.3 convert_reduce_fusion
  12.6 15.1 %all-reduce.2 = (f32[2,288]{1,0:T(2,128)S(1)}, f32[2,288]{1,0:T(2,128)S(1)}) all-reduce(f32[2,288]{1,0:T(2,128)S(1)} %get-tuple-element.6, f32[2,288]{1,0:T(2,128)S(1)} %get-tuple-element.5), channel_id=1, replica_groups=mesh['cfg'=2,'seq'=16,'wblk'=8] {'wblk'}, use_global_device_ids=true, to_apply=%region_4.5 | all-reduce | flops 1152 | bytes 9216 | tf_op jit(solution)/shard_map/psum | solution.py:141
  27.7 44.7 %psum.21 = f32[3,384]{1,0:T(4,128)S(1)} all-reduce(f32[3,384]{1,0:T(4,128)S(1)} %bitcast.105), channel_id=1, replica_groups=mesh['cfg'=2,'seq'=16,'wblk'=8] {'seq'}, use_global_device_ids=true, to_apply=%region_0.1 | all-reduce | flops 1152 | bytes 9216 | tf_op jit(solution)/shard_map/psum | solution.py:138
  72.4 2.2 broadcast_in_dim.17
  74.5 1.1 constant_dynamic-update-slice_fusion.7
  75.6 3.0 collective-permute-start.1
  78.6 6.0 %collective-permute-done = bf16[2,288,384]{2,1,0:T(8,128)(2,1)S(1)} collective-permute-done((bf16[2,288,384]{2,1,0:T(8,128)(2,1)S(1)}, bf16[2,288,384]{2,1,0:T(8,128)(2,1)S(1)}, u32[]{:S(2)}, u32[]{:S(2)}) %collective-permute-start) | collective-permute-done | bytes 442400 | tf_op jit(solution)/shard_map/ppermute | solution.py:26
  84.8 3.2 collective-permute-start.3
  88.4 5.1 collective-permute-done.2
  94.8 3.0 collective-permute-start.5
  98.7 3.8 collective-permute-done.4
  106.0 5.4 collective-permute-done.6
  112.2 12.5 %copy.34 = bf16[3072,3,2,128]{0,3,2,1:T(8,128)(2,1)} copy(bf16[3072,3,2,128]{3,2,1,0:T(2,128)(2,1)} %all-gather.8.cloned.1.call-done) | data formatting | bytes 9437184 | tf_op jit(solution)/shard_map/reshape | solution.py:96
  124.8 6.8 %fusion.6 = f32[2,288,3,2,128]{4,1,3,2,0:T(8,128)S(1)} fusion(bf16[3072,3,2,128]{0,3,2,1:T(8,128)(2,1)} %copy.34, bf16[2,288,3072]{2,1,0:T(8,128)(2,1)} %constant_dynamic-update-slice_fusion), kind=kOutput, calls=%fused_computation.8 | convolution fusion | flops 2717908992 | bytes 10027008 | tf_op jit(solution)/shard_map/dot_general | solution.py:95
  135.9 1.1 copy.27
  137.1 1.8 slice.102
  140.5 34.5 %all-gather.14.cloned.1.call-done = bf16[3072,768]{1,0:T(8,128)(2,1)} async-done(((bf16[192,768]{1,0:T(8,128)(2,1)}), bf16[3072,768]{1,0:T(8,128)(2,1)}) %all-gather.14.cloned.1.call-update) | async-done | bytes 4718608 | tf_op jit(solution)/shard_map/all_gather | solution.py:155
  175.0 83.0 %all-gather.16.cloned.1.call-done = bf16[768,3072]{0,1:T(8,128)(2,1)} async-done(((bf16[768,192]{0,1:T(8,128)(2,1)}), bf16[768,3072]{0,1:T(8,128)(2,1)}) %all-gather.16.cloned.1.call-update) | async-done | bytes 4718608 | tf_op jit(solution)/shard_map/all_gather | solution.py:203
  258.0 15.0 %fusion.39 = f32[576,3072]{1,0:T(8,128)} fusion(bf16[768,3072]{0,1:T(8,128)(2,1)} %all-gather.16.cloned.1.call-done, bf16[576,3072]{1,0:T(8,128)(2,1)} %bitcast.18, bf16[3072,768]{1,0:T(8,128)(2,1)} %all-gather.14.cloned.1.call-done), kind=kOutput, calls=%fused_computation.34 | convolution fusion | flops 5439799296 | bytes 20054016 | tf_op jit(solution)/shard_map/dot_general | solution.py:104
  273.1 68.4 %all-gather.10.cloned.1.call-done = bf16[2,4608,2,128]{3,1,2,0:T(8,128)(2,1)} async-done(((bf16[2,288,2,128]{3,1,2,0:T(8,128)(2,1)}), bf16[2,4608,2,128]{3,1,2,0:T(8,128)(2,1)}) %all-gather.10.cloned.1.call-update) | async-done | bytes 4718608 | tf_op jit(solution)/shard_map/all_gather | solution.py:172
  341.5 13.6 %fusion = (f32[2,2,288]{2,1,0:T(2,128)S(1)}, f32[2,2,288,4608]{3,2,1,0:T(8,128)}) fusion(pred[2,4608]{1,0:T(4,128)(4,1)S(1)} %compare_or_fusion, bf16[2,4608,2,128]{3,1,2,0:T(8,128)(2,1)} %all-gather.10.cloned.1.call-done, bf16[2,288,2,128]{1,2,3,0:T(2,128)(2,1)S(1)} %bitcast.100), kind=kOutput, calls=%fused_computation.2 | convolution fusion | flops 1374878592 | bytes 26260992 | tf_op jit(solution)/shard_map/pqhd,pkhd->phqk/dot_general | solution.py:181
  355.0 10.3 %fusion.1 = f32[2,2,288]{2,1,0:T(2,128)S(1)} fusion(f32[2,2,288,4608]{3,2,1,0:T(8,128)} %get-tuple-element.31, f32[2,2,288]{2,1,0:T(2,128)S(1)} %broadcast_maximum_fusion, pred[2,4608]{1,0:T(4,128)(4,1)S(1)} %compare_or_fusion), kind=kLoop, calls=%fused_computation.3 | loop fusion | flops 21232512 | bytes 21252096 | tf_op jit(solution)/shard_map/reduce_sum | solution.py:187
  365.4 59.5 %all-gather.18.cloned.1.call-done = bf16[2,4608,1,2,128]{4,1,3,2,0:T(8,128)(2,1)} async-done(((bf16[2,288,1,2,128]{4,1,3,2,0:T(8,128)(2,1)}), bf16[2,4608,1,2,128]{4,1,3,2,0:T(8,128)(2,1)}) %all-gather.18.cloned.1.call-update) | async-done | bytes 4718608 | tf_op jit(solution)/shard_map/all_gather | solution.py:173
  424.9 10.9 %fusion.28 = bf16[2,288,2,128]{3,1,2,0:T(8,128)(2,1)S(1)} fusion(bf16[2,4608,1,2,128]{4,1,3,2,0:T(8,128)(2,1)} %all-gather.18.cloned.1.call-done, f32[2,2,288,4608]{3,2,1,0:T(8,128)} %get-tuple-element.31, f32[2,2,288]{2,1,0:T(2,128)S(1)} %broadcast_maximum_fusion, pred[2,4608]{1,0:T(4,128)(4,1)S(1)} %compare_or_fusion, f32[2,288,2]{1,2,0:T(2,128)S(1)} %bitcast.106), kind=kOutput, calls=%fused_computation.27 | convolution fusion | flops 1380483072 | bytes 26265600 | tf_op jit(solution)/shard_map/phqk,pkhd->phqd/dot_general | solution.py:188
  436.0 50.0 %all-gather.12.cloned.1.call-done = bf16[256,3072]{0,1:T(8,128)(2,1)} async-done(((bf16[256,192]{0,1:T(8,128)(2,1)}), bf16[256,3072]{0,1:T(8,128)(2,1)}) %all-gather.12.cloned.1.call-update) | async-done | bytes 1572880 | tf_op jit(solution)/shard_map/all_gather | solution.py:202
  486.1 6.4 %add_convert_fusion = bf16[576,3072]{1,0:T(8,128)(2,1)} fusion(f32[576,3072]{1,0:T(8,128)} %fusion.39, bf16[256,3072]{0,1:T(8,128)(2,1)} %all-gather.12.cloned.1.call-done, bf16[72,8,2,128]{3,2,1,0:T(2,128)(2,1)S(1)} %bitcast.101), kind=kOutput, calls=%fused_computation.7 | convolution fusion | flops 909508608 | bytes 12484608 | tf_op jit(solution)/shard_map/dot_general | solution.py:103
  492.5 12.3 %copy.35 = bf16[2,288,3072]{1,0,2:T(2,128)(2,1)} copy(bf16[2,288,3072]{2,1,0:T(8,128)(2,1)} %bitcast.95) | data formatting | bytes 7077888
  504.8 10.1 %reshape.323 = bf16[3072,576]{1,0:T(8,128)(2,1)} reshape(bf16[3072,2,288]{2,1,0:T(2,128)(2,1)} %bitcast.94) | data formatting | bytes 7077888
  514.9 37.4 %reduce-scatter.4.cloned.1.call-done = bf16[384,576]{1,0:T(8,128)(2,1)} async-done(((bf16[3072,576]{1,0:T(8,128)(2,1)}), bf16[384,576]{1,0:T(8,128)(2,1)}) %reduce-scatter.4.cloned.1.call-update) | async-done | bytes 442384
  552.3 2.1 reshape.324
  556.1 3.5 all-to-all-start
  560.2 5.2 all-to-all-done
  (83 shorter events, 19.8 us)
Async XLA Ops:
  7.2 3.9 copy-start
  7.2 67.3 %copy-start.4 = (bf16[1,2,32,384]{3,2,1,0:T(8,128)(2,1)S(1)}, bf16[1,2,32,384]{3,2,1,0:T(8,128)(2,1)}, u32[]{:S(2)}) copy-start(bf16[1,2,32,384]{3,2,1,0:T(8,128)(2,1)} %param.12) | copy-start | bytes 147460
  7.2 67.3 %copy-start.2 = (bf16[2,256,384]{2,1,0:T(8,128)(2,1)S(1)}, bf16[2,256,384]{2,1,0:T(8,128)(2,1)}, u32[]{:S(2)}) copy-start(bf16[2,256,384]{2,1,0:T(8,128)(2,1)} %param.13) | copy-start | bytes 1179652
  7.2 80.9 %copy-start.5 = (f32[128]{0:T(128)S(1)}, f32[128]{0:T(128)}, u32[]{:S(2)}) copy-start(f32[128]{0:T(128)} %param.19) | copy-start | bytes 1540
  7.2 81.0 %copy-start.6 = (f32[128]{0:T(128)S(1)}, f32[128]{0:T(128)}, u32[]{:S(2)}) copy-start(f32[128]{0:T(128)} %param.18) | copy-start | bytes 1540
  7.2 105.0 %all-gather.8.cloned.1.call-start = ((), (), s32[]{:S(2)}) async-start(), calls=%async_computation.2 | async-start | bytes 5013504 | tf_op jit(solution)/shard_map/all_gather | solution.py:154
  8.0 167.1 %all-gather.14.cloned.1.call-start = ((), (), s32[]{:S(2)}) async-start(), calls=%async_computation.5 | async-start | bytes 5013504 | tf_op jit(solution)/shard_map/all_gather | solution.py:155
  8.7 249.3 %all-gather.16.cloned.1.call-start = ((), (), s32[]{:S(2)}) async-start(), calls=%async_computation.6 | async-start | bytes 5013504 | tf_op jit(solution)/shard_map/all_gather | solution.py:203
  9.4 332.0 %all-gather.10.cloned.1.call-start = ((), (), s32[]{:S(2)}) async-start(), calls=%async_computation.3 | async-start | bytes 5013504 | tf_op jit(solution)/shard_map/all_gather | solution.py:172
  75.6 8.9 %collective-permute-start = (bf16[2,288,384]{2,1,0:T(8,128)(2,1)S(1)}, bf16[2,288,384]{2,1,0:T(8,128)(2,1)S(1)}, u32[]{:S(2)}, u32[]{:S(2)}) collective-permute-start(bf16[2,288,384]{2,1,0:T(8,128)(2,1)S(1)} %get-tuple-element.15), channel_id=1, source_target_pairs={{0,1},{1,2},{2,3},{3,4},{4,5},{5,6},{6,7},{7,0},{8,9},{9,10},{10,1... | collective-permute-start | bytes 1327112 | tf_op jit(solution)/shard_map/ppermute | solution.py:26
  75.6 9.1 %collective-permute-start.1 = (bf16[2,288,384]{2,1,0:T(8,128)(2,1)S(1)}, bf16[2,288,384]{2,1,0:T(8,128)(2,1)S(1)}, u32[]{:S(2)}, u32[]{:S(2)}) collective-permute-start(bf16[2,288,384]{2,1,0:T(8,128)(2,1)S(1)} %get-tuple-element.15), channel_id=1, source_target_pairs={{0,7},{1,0},{2,1},{3,2},{4,3},{5,4},{6,5},{7,6},{8,15},{9,8},{10,9... | collective-permute-start | bytes 1327112 | tf_op jit(solution)/shard_map/ppermute | solution.py:29
  84.6 8.9 %collective-permute-start.2 = (bf16[2,288,384]{2,1,0:T(8,128)(2,1)S(1)}, bf16[2,288,384]{2,1,0:T(8,128)(2,1)S(1)}, u32[]{:S(2)}, u32[]{:S(2)}) collective-permute-start(bf16[2,288,384]{2,1,0:T(8,128)(2,1)S(1)} %collective-permute-done), channel_id=1, source_target_pairs={{0,1},{1,2},{2,3},{3,4},{4,5},{5,6},{6,7},{7,0},{8,9},{9,10},{10,1... | collective-permute-start | bytes 1327112 | tf_op jit(solution)/shard_map/ppermute | solution.py:26
  84.8 10.0 %collective-permute-start.3 = (bf16[2,288,384]{2,1,0:T(8,128)(2,1)S(1)}, bf16[2,288,384]{2,1,0:T(8,128)(2,1)S(1)}, u32[]{:S(2)}, u32[]{:S(2)}) collective-permute-start(bf16[2,288,384]{2,1,0:T(8,128)(2,1)S(1)} %collective-permute-done.1), channel_id=1, source_target_pairs={{0,7},{1,0},{2,1},{3,2},{4,3},{5,4},{6,5},{7,6},{8,15},{9,8},{10,9... | collective-permute-start | bytes 1327112 | tf_op jit(solution)/shard_map/ppermute | solution.py:29
  93.5 8.9 %collective-permute-start.4 = (bf16[2,288,384]{2,1,0:T(8,128)(2,1)S(1)}, bf16[2,288,384]{2,1,0:T(8,128)(2,1)S(1)}, u32[]{:S(2)}, u32[]{:S(2)}) collective-permute-start(bf16[2,288,384]{2,1,0:T(8,128)(2,1)S(1)} %collective-permute-done.2), channel_id=1, source_target_pairs={{0,1},{1,2},{2,3},{3,4},{4,5},{5,6},{6,7},{7,0},{8,9},{9,10},{10,1... | collective-permute-start | bytes 1327112 | tf_op jit(solution)/shard_map/ppermute | solution.py:26
  94.8 10.3 %collective-permute-start.5 = (bf16[2,288,384]{2,1,0:T(8,128)(2,1)S(1)}, bf16[2,288,384]{2,1,0:T(8,128)(2,1)S(1)}, u32[]{:S(2)}, u32[]{:S(2)}) collective-permute-start(bf16[2,288,384]{2,1,0:T(8,128)(2,1)S(1)} %collective-permute-done.3), channel_id=1, source_target_pairs={{0,7},{1,0},{2,1},{3,2},{4,3},{5,4},{6,5},{7,6},{8,15},{9,8},{10,9... | collective-permute-start | bytes 1327112 | tf_op jit(solution)/shard_map/ppermute | solution.py:29
  102.4 8.9 %collective-permute-start.6 = (bf16[2,288,384]{2,1,0:T(8,128)(2,1)S(1)}, bf16[2,288,384]{2,1,0:T(8,128)(2,1)S(1)}, u32[]{:S(2)}, u32[]{:S(2)}) collective-permute-start(bf16[2,288,384]{2,1,0:T(8,128)(2,1)S(1)} %collective-permute-done.4), channel_id=1, source_target_pairs={{0,1},{1,2},{2,3},{3,4},{4,5},{5,6},{6,7},{7,0},{8,9},{9,10},{10,1... | collective-permute-start | bytes 1327112 | tf_op jit(solution)/shard_map/ppermute | solution.py:26
  131.5 1.2 copy-start.3
  133.2 6.6 %copy-start.7 = (s32[2]{0:T(128)S(1)}, s32[2]{0:T(128)}, u32[]{:S(2)}) copy-start(s32[2]{0:T(128)} %param.22) | copy-start | bytes 28
  137.1 287.8 %all-gather.18.cloned.1.call-start = ((), (), s32[]{:S(2)}) async-start(), calls=%async_computation.7 | async-start | bytes 5013504 | tf_op jit(solution)/shard_map/all_gather | solution.py:173
  139.0 347.1 %all-gather.12.cloned.1.call-start = ((), (), s32[]{:S(2)}) async-start(), calls=%async_computation.4 | async-start | bytes 1671168 | tf_op jit(solution)/shard_map/all_gather | solution.py:202
  139.5 412.8 %reduce-scatter.4.cloned.1.call-start = ((), (), s32[]{:S(2)}) async-start(), calls=%async_computation.8 | async-start | bytes 4423680
  514.9 51.5 %copy-start.1 = (bf16[192,3,384]{2,0,1:T(8,128)(2,1)S(1)}, bf16[192,3,384]{2,0,1:T(8,128)(2,1)}, u32[]{:S(2)}) copy-start(bf16[192,3,384]{2,0,1:T(8,128)(2,1)} %param.15) | copy-start | bytes 1327108
  556.1 9.3 %all-to-all-start = ((bf16[2,1,256,384]{3,2,1,0:T(8,128)(2,1)}), bf16[2,1,256,384]{3,2,1,0:T(8,128)(2,1)S(1)}, u32[]{:S(2)}, u32[]{:S(2)}) async-start(bf16[2,1,256,384]{3,2,1,0:T(8,128)(2,1)} %slice_bitcast_fusion.2), calls=%async_computation | async-start | bytes 786432 | tf_op jit(solution)/shard_map/all_to_all | solution.py:215
Sparse Core Ops, SparseCore 0:
  10.5 81.4 all-gather.7
  94.4 80.5 all-gather.13
  177.5 80.5 all-gather.15
  260.9 80.5 all-gather.9
  344.3 80.5 all-gather.17
  427.2 58.8 all-gather.11
  515.1 37.2 reduce-scatter.3
